TPU v7x, 32 devices: a whole 2x2x4 slice. The times are simulated.
32 devices in a mesh: row: 4 (over y, core), col: 8 (over z, x).
Axes of the slice: x: 2, y: 2, z: 4, core: 2. Of those that a mesh axis runs over, the one named last changes fastest.
Arguments:
- node_feats: bfloat16 [8192, 256], P(('row', 'col')), may hold values from -6 to 6
- weight: bfloat16 [256, 256], replicated, may hold values from -0.375 to 0.375
- cotangent: bfloat16 [8192, 256], P(('row', 'col')), may hold values from -6 to 6
- band_tiles: bfloat16 [384, 128, 128], P(('row', 'col')), may hold values from 0 to 0.049804688
- band_coords: int32 [384, 2], P(('row', 'col')), may hold values from 0 to 5, as said below
- bound_tiles: bfloat16 [1280, 128, 128], P(('row', 'col')), may hold values from 0 to 0.049804688
- bound_coords: int32 [1280, 2], P(('row', 'col')), may hold values from 0 to 7, as said below
- bound_count: int32 [32], P(('row', 'col')), may hold values from 0 to 40, as said below
- recv_lists: int32 [32, 8], P(('row', 'col')), may hold values from -1 to 1, as said below
- send_lists: int32 [32, 8], P(('row', 'col')), may hold values from -1 to 1, as said below
- reorder: int32 [32, 256], P(('row', 'col')), may hold values from 0 to 255, each once within a row
Outputs:
- node_out: bfloat16 [8192, 256], P(('row', 'col'))
- feat_grad: bfloat16 [8192, 256], P(('row', 'col'))
- weight_grad: float32 [256, 256], replicated
Inputs may be any that keep to these rules, and one draw needn't show every extreme that they name: recv_lists[r * 8 + c, s] is a row block of device r * 8 + s, below 2, or -1 for none; it is -1 where s = c. In every row group one device receives a block from every other column. send_lists[r * 8 + s, c] equals recv_lists[r * 8 + c, s]. bound_count[d] is at least the number of entries of recv_lists[d] that are not -1; in every row group one device has all 40 slots live. `bound_coords`: pairs (row block below 2, owner column below 8); for k < bound_count[d] the owner column s of slot k has recv_lists[d, s] >= 0, and every such column is named by one of them; slots from bound_count[d] on are not used. `band_coords`: pairs (row block below 2, extended column block below (768) / 128); no pair twice on one device. `reorder`: each row is a permutation.
All inputs are finite; a program needn't handle non-finite values.
Results may differ from a plain program's by a relative error of at most 0.0095.
Values may be sent and summed in bfloat16 or wider, within the bound.
No kernel may reach another device: no remote copies, remote signals or barrier semaphores. Data moves between devices by JAX's collectives and lax.ppermute only.
A program may use at most 64 MiB of HBM per device.

v0:
```python
import jax
import jax.numpy as jnp
from jax import lax
from jax.sharding import PartitionSpec as P

BW = 256


def padded_2(cells, sides, width):
    for axis, dim in sides:
        count = lax.axis_size(axis)
        head = lax.slice_in_dim(cells, 0, width, axis=dim)
        tail = lax.slice_in_dim(cells, cells.shape[dim] - width, cells.shape[dim], axis=dim)
        cells = jnp.concatenate(
            [
                lax.ppermute(tail, axis, [(i, (i + 1) % count) for i in range(count)]),
                cells,
                lax.ppermute(head, axis, [((i + 1) % count, i) for i in range(count)]),
            ],
            axis=dim,
        )
    return cells


def split_sum(selector, terms):
    high_part = terms.astype(jnp.bfloat16)
    low_part = (terms - high_part.astype(jnp.float32)).astype(jnp.bfloat16)
    pick = selector.astype(jnp.bfloat16)
    upper_sum = jnp.einsum("rk,kaf->raf", pick, high_part, preferred_element_type=jnp.float32)
    lower_sum = jnp.einsum("rk,kaf->raf", pick, low_part, preferred_element_type=jnp.float32)
    return upper_sum + lower_sum


def on_device(
    node_feats,
    weight,
    cotangent,
    band_tiles,
    band_coords,
    bound_tiles,
    bound_coords,
    bound_count,
    recv_lists,
    send_lists,
    reorder,
):
    tile_size = band_tiles.shape[1]
    row_count = node_feats.shape[0]
    width_feat = node_feats.shape[1]
    tile_rows = row_count // tile_size
    rim_tiles = BW // tile_size
    col_tiles = tile_rows + 2 * rim_tiles
    ext_count = row_count + 2 * BW
    peers = lax.axis_size("col")
    slot_total = bound_tiles.shape[0]
    order = reorder[0]
    inverse = (
        jnp.zeros((row_count,), jnp.int32).at[order].set(jnp.arange(row_count, dtype=jnp.int32))
    )
    x_band = jnp.take(node_feats, order, axis=0)
    hidden = jnp.dot(x_band, weight, preferred_element_type=jnp.float32).astype(jnp.bfloat16)
    band_row_ids = band_coords[:, 0]
    band_col_ids = band_coords[:, 1]
    band_dense = jnp.zeros((tile_rows, tile_size, col_tiles, tile_size), jnp.bfloat16)
    band_dense = (
        band_dense.at[band_row_ids, :, band_col_ids].set(band_tiles).reshape(row_count, ext_count)
    )
    extended = padded_2(hidden, (("row", 0),), BW)
    mixed = jnp.dot(band_dense, extended, preferred_element_type=jnp.float32)
    blocks = hidden.reshape(tile_rows, tile_size, width_feat)
    giving = send_lists[0]
    outgoing = jnp.where(
        (giving >= 0)[:, None, None],
        jnp.take(blocks, jnp.maximum(giving, 0), axis=0),
        jnp.zeros((), jnp.bfloat16),
    )
    arrived = lax.all_to_all(outgoing, "col", split_axis=0, concat_axis=0, tiled=True)
    tile_range = jnp.arange(tile_rows, dtype=jnp.int32)
    live_slots = jnp.arange(slot_total, dtype=jnp.int32) < bound_count[0]
    bound_row_ids = bound_coords[:, 0]
    bound_owner = bound_coords[:, 1]
    bound_onehot = (bound_row_ids[None, :] == tile_range[:, None]) & live_slots[None, :]
    slot_rows = jnp.take(arrived, bound_owner, axis=0).reshape(slot_total * tile_size, width_feat)
    placed = jnp.einsum(
        "rk,kab->rakb",
        bound_onehot.astype(jnp.bfloat16),
        bound_tiles,
        preferred_element_type=jnp.bfloat16,
    )
    placed = placed.reshape(row_count, slot_total * tile_size)
    mixed = mixed + jnp.dot(placed, slot_rows, preferred_element_type=jnp.float32)
    out_band = jax.nn.silu(mixed).astype(jnp.bfloat16)
    node_out = jnp.take(out_band, inverse, axis=0)
    grad_band = jnp.take(cotangent, order, axis=0).astype(jnp.float32)
    sigma = jax.nn.sigmoid(mixed)
    slope = (grad_band * sigma * (1.0 + mixed * (1.0 - sigma))).astype(jnp.bfloat16)
    slope_blocks = slope.reshape(tile_rows, tile_size, width_feat)
    ext_grad = lax.dot_general(
        band_dense, slope, (((0,), (0,)), ((), ())), preferred_element_type=jnp.float32
    )
    rim_terms = jnp.concatenate([ext_grad[:BW], ext_grad[BW + row_count :]], axis=0).astype(
        jnp.bfloat16
    )
    padded = padded_2(rim_terms, (("row", 0),), BW)
    grad_hidden = ext_grad[BW : BW + row_count]
    grad_hidden = grad_hidden.at[:BW].add(padded[:BW].astype(jnp.float32))
    grad_hidden = grad_hidden.at[row_count - BW :].add(padded[3 * BW :].astype(jnp.float32))
    slot_back = jnp.einsum(
        "kab,kaf->kbf",
        bound_tiles,
        jnp.take(slope_blocks, bound_row_ids, axis=0),
        preferred_element_type=jnp.float32,
    )
    owner_range = jnp.arange(peers, dtype=jnp.int32)
    owner_onehot = (bound_owner[None, :] == owner_range[:, None]) & live_slots[None, :]
    to_owner = split_sum(owner_onehot, slot_back).astype(jnp.bfloat16)
    returned = lax.all_to_all(to_owner, "col", split_axis=0, concat_axis=0, tiled=True)
    block_onehot = (giving[None, :] == tile_range[:, None]).astype(jnp.bfloat16)
    from_peers = jnp.einsum(
        "bs,saf->baf", block_onehot, returned, preferred_element_type=jnp.float32
    )
    grad_hidden = grad_hidden + from_peers.reshape(row_count, width_feat)
    grad_round = grad_hidden.astype(jnp.bfloat16)
    partial_weight = lax.dot_general(
        x_band, grad_round, (((0,), (0,)), ((), ())), preferred_element_type=jnp.float32
    )
    nodes_all = row_count * lax.axis_size("row") * peers
    weight_grad = lax.psum(partial_weight, ("row", "col")) * nodes_all ** (-0.5)
    feat_band = lax.dot_general(
        grad_round, weight, (((1,), (1,)), ((), ())), preferred_element_type=jnp.float32
    ).astype(jnp.bfloat16)
    feat_grad = jnp.take(feat_band, inverse, axis=0)
    return (node_out, feat_grad, weight_grad)


def solution(mesh):
    in_specs = (
        P(("row", "col"), None),
        P(),
        P(("row", "col"), None),
        P(("row", "col"), None, None),
        P(("row", "col"), None),
        P(("row", "col"), None, None),
        P(("row", "col"), None),
        P(("row", "col")),
        P(("row", "col"), None),
        P(("row", "col"), None),
        P(("row", "col"), None),
    )
    out_specs = (P(("row", "col"), None), P(("row", "col"), None), P())
    return jax.shard_map(
        on_device, mesh=mesh, in_specs=in_specs, out_specs=out_specs, check_vma=False
    )
```

profile of v0, /device:TPU:0, one launch (start us, length us, event | category | flops | bytes accessed | tf_op | source)
XLA Modules:
  0.0 214.7 jit_solution(14946147041477789685)
XLA Ops:
  7.2 0.8 compare_select_fusion.2
  8.0 0.7 compare_and_fusion.1
  8.7 1.9 gather_fusion.3
  11.4 2.0 collective-permute-start.1
  15.3 0.9 select_select_fusion
  16.3 6.5 %all-to-all-start = ((bf16[8,128,256]{2,1,0:T(8,128)(2,1)}), bf16[8,128,256]{2,1,0:T(8,128)(2,1)S(1)}, u32[]{:S(2)}, u32[]{:S(2)}) async-start(bf16[8,128,256]{2,1,0:T(8,128)(2,1)} %select_select_fusion), calls=%async_computation | async-start | bytes 1048576 | tf_op jit(solution)/shard_map/all_to_all | solution.py:77
  25.2 0.8 copy.20
  26.1 1.8 gather_fusion.5
  28.0 2.0 scatter_fusion
  30.1 1.1 copy.19
  31.2 2.1 scatter_custom_fusion.1
  33.8 1.7 broadcast_multiply_fusion
  35.6 1.8 all-to-all-done
  37.3 0.7 gather_fusion.1
  38.4 1.4 copy-done.4
  39.8 0.8 fusion.1
  40.8 1.3 multiply_convert_fusion
  42.2 2.4 %gather_fusion.2 = bf16[40,128,256]{2,1,0:T(8,128)(2,1)} fusion(bf16[2,128,256]{2,1,0:T(8,128)(2,1)S(1)} %bitcast.73, s32[1024]{0:T(1024)S(1)} %pad_clamp_fusion), kind=kCustom, calls=%fused_computation.6 | custom fusion | bytes 5243040 | tf_op jit(solution)/shard_map/jit(_take)/gather | solution.py:111
  44.6 4.9 %fusion = (bf16[40,128,256]{1,2,0:T(8,128)(2,1)S(1)}, bf16[40,128,256]{1,2,0:T(8,128)(2,1)}) fusion(bf16[40,128,128]{2,1,0:T(8,128)(2,1)} %param.26, bf16[40,128,256]{2,1,0:T(8,128)(2,1)} %gather_fusion.2, pred[40]{0:T(512)(128)(4,1)S(1)} %copy-done.16), kind=kOutput, calls=%fused_computation.11 | convolution fusion | flops 342097920 | bytes 9175080 | tf_op jit(solution)/shard_map/kab,kaf->kbf/dot_general | solution.py:108
  49.5 4.7 %copy.22 = bf16[40,128,256]{2,0,1:T(8,128)(2,1)} copy(bf16[40,128,256]{1,2,0:T(8,128)(2,1)} %get-tuple-element.45) | data formatting | bytes 5242880 | tf_op jit(solution)/shard_map/convert_element_type | solution.py:26
  54.2 3.4 %copy.23 = bf16[40,128,256]{2,0,1:T(8,128)(2,1)} copy(bf16[40,128,256]{1,2,0:T(8,128)(2,1)S(1)} %get-tuple-element.44) | data formatting | bytes 5242880 | tf_op jit(solution)/shard_map/convert_element_type | solution.py:27
  57.6 2.5 %fusion.28 = f32[8,128,256]{2,0,1:T(8,128)S(1)} fusion(bf16[40,128,256]{2,0,1:T(8,128)(2,1)} %copy.22, s32[40]{0:T(128)S(1)} %get-tuple-element.50, pred[40]{0:T(512)(128)(4,1)S(1)} %copy-done.15), kind=kOutput, calls=%fused_computation.62 | convolution fusion | flops 20972160 | bytes 3670216 | tf_op jit(solution)/shard_map/rk,kaf->raf/dot_general | solution.py:29
  60.7 0.9 copy.24
  61.6 4.2 %all-to-all-start.1 = ((bf16[8,128,256]{2,1,0:T(8,128)(2,1)}), bf16[8,128,256]{2,1,0:T(8,128)(2,1)S(1)}, u32[]{:S(2)}, u32[]{:S(2)}) async-start(bf16[8,128,256]{2,1,0:T(8,128)(2,1)} %copy.24), calls=%async_computation.1 | async-start | bytes 1048576 | tf_op jit(solution)/shard_map/all_to_all | solution.py:117
  66.3 1.7 collective-permute-start.3
  68.0 1.1 gather_fusion.4
  69.2 10.8 %all-to-all-done.1 = bf16[8,128,256]{2,1,0:T(8,128)(2,1)S(1)} async-done(((bf16[8,128,256]{2,1,0:T(8,128)(2,1)}), bf16[8,128,256]{2,1,0:T(8,128)(2,1)S(1)}, u32[]{:S(2)}, u32[]{:S(2)}) %all-to-all-start.1) | async-done | bytes 524320 | tf_op jit(solution)/shard_map/all_to_all | solution.py:117
  80.7 1.0 fusion.24
  81.7 1.1 gather_fusion.6
  82.9 0.8 broadcast_select_fusion.1
  83.7 122.5 %all-reduce.2.cloned.1.call-done = f32[256,256]{1,0:T(8,128)} async-done(((f32[256,256]{1,0:T(8,128)}), f32[256,256]{1,0:T(8,128)}) %all-reduce.2.cloned.1.call-update) | async-done | bytes 262160 | tf_op jit(solution)/shard_map/psum | solution.py:128
  206.1 1.7 broadcast_multiply_fusion.1
  (78 shorter events, 7.3 us)
Async XLA Ops:
  7.2 3.4 %copy-start = (bf16[256,256]{1,0:T(8,128)(2,1)S(1)}, bf16[256,256]{1,0:T(8,128)(2,1)}, u32[]{:S(2)}) copy-start(bf16[256,256]{1,0:T(8,128)(2,1)} %param.22) | copy-start | bytes 393220
  7.2 15.6 %copy-start.11 = (s32[1,256]{1,0:T(1,128)S(1)}, s32[1,256]{1,0:T(1,128)}, u32[]{:S(2)}) copy-start(s32[1,256]{1,0:T(1,128)} %param.30) | copy-start | bytes 3076
  7.2 16.2 %copy-start.9 = (s32[40,2]{0,1:T(2,128)S(1)}, s32[40,2]{0,1:T(2,128)}, u32[]{:S(2)}) copy-start(s32[40,2]{0,1:T(2,128)} %param.27) | copy-start | bytes 964
  7.2 17.4 %copy-start.21 = (s32[12,2]{0,1:T(2,128)S(1)}, s32[12,2]{0,1:T(2,128)}, u32[]{:S(2)}) copy-start(s32[12,2]{0,1:T(2,128)} %param.25) | copy-start | bytes 292
  7.2 18.0 %copy-start.3 = (bf16[40,128,128]{2,1,0:T(8,128)(2,1)S(1)}, bf16[40,128,128]{2,1,0:T(8,128)(2,1)}, u32[]{:S(2)}) copy-start(bf16[40,128,128]{2,1,0:T(8,128)(2,1)} %param.26) | copy-start | bytes 3932164
  8.7 5.3 %copy-start.12 = (pred[256]{0:T(512)(128)(4,1)}, pred[256]{0:T(512)(128)(4,1)S(1)}, u32[]{:S(2)}) copy-start(pred[256]{0:T(512)(128)(4,1)S(1)} %compare_and_fusion.1) | copy-start | bytes 772
  10.6 4.1 %copy-start.6 = (bf16[256,256]{1,0:T(8,128)(2,1)}, bf16[256,256]{1,0:T(8,128)(2,1)S(1)}, u32[]{:S(2)}) copy-start(bf16[256,256]{1,0:T(8,128)(2,1)S(1)} %gather_fusion.3) | copy-start | bytes 393220
  10.9 29.8 %collective-permute-start = (bf16[256,256]{1,0:T(8,128)(2,1)S(1)}, bf16[256,256]{1,0:T(8,128)(2,1)}, u32[]{:S(2)}, u32[]{:S(2)}) collective-permute-start(bf16[256,256]{1,0:T(8,128)(2,1)S(1)} %convolution_convert_fusion.1), channel_id=1, source_target_pairs={{0,8},{8,16},{16,24},{24,0},{1,9},{9,17},{17,25},{25,1},{2,10},{10... | collective-permute-start | bytes 393224 | tf_op jit(solution)/shard_map/ppermute | solution.py:16
  11.4 29.3 %collective-permute-start.1 = (bf16[256,256]{1,0:T(8,128)(2,1)S(1)}, bf16[256,256]{1,0:T(8,128)(2,1)}, u32[]{:S(2)}, u32[]{:S(2)}) collective-permute-start(bf16[256,256]{1,0:T(8,128)(2,1)S(1)} %convolution_convert_fusion.1), channel_id=1, source_target_pairs={{8,0},{16,8},{24,16},{0,24},{9,1},{17,9},{25,17},{1,25},{10,2},{18... | collective-permute-start | bytes 393224 | tf_op jit(solution)/shard_map/ppermute | solution.py:18
  15.3 10.8 %copy-start.2 = (bf16[256,256]{1,0:T(8,128)(2,1)S(1)}, bf16[256,256]{1,0:T(8,128)(2,1)}, u32[]{:S(2)}) copy-start(bf16[256,256]{1,0:T(8,128)(2,1)} %param.23) | copy-start | bytes 393220
  16.3 21.1 %all-to-all-start = ((bf16[8,128,256]{2,1,0:T(8,128)(2,1)}), bf16[8,128,256]{2,1,0:T(8,128)(2,1)S(1)}, u32[]{:S(2)}, u32[]{:S(2)}) async-start(bf16[8,128,256]{2,1,0:T(8,128)(2,1)} %select_select_fusion), calls=%async_computation | async-start | bytes 1048576 | tf_op jit(solution)/shard_map/all_to_all | solution.py:77
  26.1 7.2 %copy-start.17 = (s32[40]{0:T(128)S(1)}, s32[40]{0:T(128)}, u32[]{:S(2)}) copy-start(s32[40]{0:T(128)} %get-tuple-element.51) | copy-start | bytes 484
  26.1 7.2 %copy-start.14 = (pred[40]{0:T(512)(128)(4,1)S(1)}, pred[40]{0:T(512)(128)(4,1)}, u32[]{:S(2)}) copy-start(pred[40]{0:T(512)(128)(4,1)} %iota_compare_fusion.1) | copy-start | bytes 124
  26.1 7.2 %copy-start.19 = (s32[40]{0:T(128)S(1)}, s32[40]{0:T(128)}, u32[]{:S(2)}) copy-start(s32[40]{0:T(128)} %get-tuple-element.53) | copy-start | bytes 484
  26.1 7.2 %copy-start.10 = (s32[40,2]{0,1:T(2,128)S(1)}, s32[40,2]{0,1:T(2,128)}, u32[]{:S(2)}) copy-start(s32[40,2]{0,1:T(2,128)} %param.27) | copy-start | bytes 964
  38.1 1.7 copy-start.4
  39.8 1.0 copy-start.5
  39.8 1.0 copy-start.8
  39.8 1.0 copy-start.13
  42.2 2.4 %copy-start.16 = (pred[40]{0:T(512)(128)(4,1)S(1)}, pred[40]{0:T(512)(128)(4,1)}, u32[]{:S(2)}) copy-start(pred[40]{0:T(512)(128)(4,1)} %get-tuple-element.54) | copy-start | bytes 124
  54.2 3.4 %copy-start.15 = (pred[40]{0:T(512)(128)(4,1)S(1)}, pred[40]{0:T(512)(128)(4,1)}, u32[]{:S(2)}) copy-start(pred[40]{0:T(512)(128)(4,1)} %iota_compare_fusion.1) | copy-start | bytes 124
  57.6 2.5 %copy-start.1 = (bf16[40,128,256]{2,0,1:T(8,128)(2,1)S(1)}, bf16[40,128,256]{2,0,1:T(8,128)(2,1)}, u32[]{:S(2)}) copy-start(bf16[40,128,256]{2,0,1:T(8,128)(2,1)} %copy.23) | copy-start | bytes 7864324
  60.1 5.8 %copy-start.18 = (s32[256]{0:T(256)S(1)}, s32[256]{0:T(256)}, u32[]{:S(2)}) copy-start(s32[256]{0:T(256)} %scatter_custom_fusion.1) | copy-start | bytes 3076
  60.7 19.3 %copy-start.20 = (s32[1,8]{1,0:T(1,128)S(1)}, s32[1,8]{1,0:T(1,128)}, u32[]{:S(2)}) copy-start(s32[1,8]{1,0:T(1,128)} %param.29) | copy-start | bytes 100
  61.6 18.4 %all-to-all-start.1 = ((bf16[8,128,256]{2,1,0:T(8,128)(2,1)}), bf16[8,128,256]{2,1,0:T(8,128)(2,1)S(1)}, u32[]{:S(2)}, u32[]{:S(2)}) async-start(bf16[8,128,256]{2,1,0:T(8,128)(2,1)} %copy.24), calls=%async_computation.1 | async-start | bytes 1048576 | tf_op jit(solution)/shard_map/all_to_all | solution.py:117
  65.8 140.3 %all-reduce.2.cloned.1.call-start = ((), (), s32[]{:S(2)}) async-start(), calls=%async_computation.2 | async-start | bytes 524288 | tf_op jit(solution)/shard_map/psum | solution.py:128
  65.9 14.8 %copy-start.7 = (bf16[256,256]{1,0:T(8,128)(2,1)S(1)}, bf16[256,256]{1,0:T(8,128)(2,1)}, u32[]{:S(2)}) copy-start(bf16[256,256]{1,0:T(8,128)(2,1)} %copy-done.6) | copy-start | bytes 393220
  66.2 14.1 %collective-permute-start.2 = (bf16[256,256]{1,0:T(8,128)(2,1)S(1)}, bf16[256,256]{1,0:T(8,128)(2,1)S(1)}, u32[]{:S(2)}, u32[]{:S(2)}) collective-permute-start(bf16[256,256]{1,0:T(8,128)(2,1)S(1)} %get-tuple-element.46), channel_id=1, source_target_pairs={{0,8},{8,16},{16,24},{24,0},{1,9},{9,17},{17,25},{25,1},{2,10},{10... | collective-permute-start | bytes 393224 | tf_op jit(solution)/shard_map/ppermute | solution.py:16
  66.3 14.1 %collective-permute-start.3 = (bf16[256,256]{1,0:T(8,128)(2,1)S(1)}, bf16[256,256]{1,0:T(8,128)(2,1)S(1)}, u32[]{:S(2)}, u32[]{:S(2)}) collective-permute-start(bf16[256,256]{1,0:T(8,128)(2,1)S(1)} %get-tuple-element.47), channel_id=1, source_target_pairs={{8,0},{16,8},{24,16},{0,24},{9,1},{17,9},{25,17},{1,25},{10,2},{18... | collective-permute-start | bytes 393224 | tf_op jit(solution)/shard_map/ppermute | solution.py:18
Sparse Core Ops, SparseCore 0:
  83.0 123.1 all-reduce.1
where the time goes:
time: 215 us
  waiting for transfers between devices  135 us (63%)
  local copies, waits for them, and re-layouts  26.5 us (12%)
  starting transfers between devices  15.1 us (7%)
  between operations  15.1 us (7%)
  matrix products  12.3 us (6%)
  other arithmetic  10.6 us (5%)
    psum x1, waiting for transfers between devices, on_device(): weight_grad = lax.psum(partial_weight, ('row', 'col')) * nodes_all ** (-0.5)  122 us
    all_to_all x1, waiting for transfers between devices, on_device(): lax.all_to_all(to_owner, 'col', split_axis=0, concat_axis=0, tiled=True)  10.8 us
    all_to_all x1, starting transfers between devices, on_device(): lax.all_to_all(outgoing, 'col', split_axis=0, concat_axis=0, tiled=True)  6.53 us
    dot_general x1, matrix products, on_device(): jnp.einsum('kab,kaf->kbf', bound_tiles, jnp.take(slope_blocks, bound_row_...  4.94 us
    convert_element_type x1, local copies, waits for them, and re-layouts, split_sum(): high_part = terms.astype(jnp.bfloat16)  4.69 us
  transfers between devices with their start and end apart: 7, of which 3 were waited for; matrix products, arithmetic and copies ran while one was open for 9% of the time, Pallas kernels for 0%

commit v1 on v0

--- a/solution.py
+++ b/solution.py
@@ -4,6 +4,9 @@
 from jax.sharding import PartitionSpec as P
 
 BW = 256
+switch_the_plane = lambda axis_id, vector: jnp.sum(
+    lax.all_gather(vector, axis_name=axis_id), axis=0
+)
 
 
 def padded_2(cells, sides, width):
@@ -125,7 +128,7 @@
         x_band, grad_round, (((0,), (0,)), ((), ())), preferred_element_type=jnp.float32
     )
     nodes_all = row_count * lax.axis_size("row") * peers
-    weight_grad = lax.psum(partial_weight, ("row", "col")) * nodes_all ** (-0.5)
+    weight_grad = switch_the_plane(("row", "col"), partial_weight) * nodes_all ** (-0.5)
     feat_band = lax.dot_general(
         grad_round, weight, (((1,), (1,)), ((), ())), preferred_element_type=jnp.float32
     ).astype(jnp.bfloat16)

time: 215 us -> 169 us (0.79)
  waiting for transfers between devices: 135 us -> 87.9 us
  other arithmetic: 10.6 us -> 13 us
    psum x1 -> x0, waiting for transfers between devices: 122 us -> none  [on_device(): weight_grad = lax.psum(partial_weight, ('row', 'col')) * nodes_all ** (-0.5)]
    all_gather x0 -> x1, waiting for transfers between devices: none -> 70.9 us  [lax.all_gather(vector, axis_name=axis_id)]
    reduce_sum x0 -> x1, other arithmetic: none -> 3.93 us  [jnp.sum(lax.all_gather(vector, axis_name=axis_id), axis=0)]
    all_to_all x1, waiting for transfers between devices: 1.76 us -> 4.48 us  [on_device(): lax.all_to_all(outgoing, 'col', split_axis=0, concat_axis=0, tiled=True)]
  transfers between devices with their start and end apart: 7 -> 7, of which waited for: 3 -> 3; matrix products, arithmetic and copies ran while one was open for 9% -> 12% of each run, Pallas kernels for 0% -> 0%
where the time goes in v1:
time: 169 us
  waiting for transfers between devices  87.9 us (52%)
  local copies, waits for them, and re-layouts  25.9 us (15%)
  between operations  15.1 us (9%)
  starting transfers between devices  14.7 us (9%)
  other arithmetic  13 us (8%)
  matrix products  12.3 us (7%)
    all_gather x1, waiting for transfers between devices, lax.all_gather(vector, axis_name=axis_id)  70.9 us
    all_to_all x1, waiting for transfers between devices, on_device(): lax.all_to_all(to_owner, 'col', split_axis=0, concat_axis=0, tiled=True)  12.5 us
    all_to_all x1, starting transfers between devices, on_device(): lax.all_to_all(outgoing, 'col', split_axis=0, concat_axis=0, tiled=True)  6.53 us
    dot_general x1, matrix products, on_device(): jnp.einsum('kab,kaf->kbf', bound_tiles, jnp.take(slope_blocks, bound_row_...  4.95 us
    convert_element_type x1, local copies, waits for them, and re-layouts, split_sum(): high_part = terms.astype(jnp.bfloat16)  4.74 us
    all_to_all x1, waiting for transfers between devices, on_device(): lax.all_to_all(outgoing, 'col', split_axis=0, concat_axis=0, tiled=True)  4.48 us
    reduce_sum x1, other arithmetic, jnp.sum(lax.all_gather(vector, axis_name=axis_id), axis=0)  3.93 us
    all_to_all x1, starting transfers between devices, on_device(): lax.all_to_all(to_owner, 'col', split_axis=0, concat_axis=0, tiled=True)  3.77 us
  transfers between devices with their start and end apart: 7, of which 3 were waited for; matrix products, arithmetic and copies ran while one was open for 12% of the time, Pallas kernels for 0%

profile of v1, /device:TPU:0, one launch (start us, length us, event | category | flops | bytes accessed | tf_op | source)
XLA Modules:
  0.0 168.8 jit_solution(10497190896674607106)
XLA Ops:
  7.2 0.8 compare_select_fusion.2
  8.7 1.9 %gather_fusion.3 = bf16[256,256]{1,0:T(8,128)(2,1)S(1)} fusion(bf16[256,256]{1,0:T(8,128)(2,1)} %param.21, s32[1024]{0:T(1024)S(1)} %pad_clamp_fusion.4), kind=kCustom, calls=%fused_computation.clone | custom fusion | bytes 263168 | tf_op jit(solution)/shard_map/jit(_take)/gather | solution.py:63
  11.4 2.0 %collective-permute-start.1 = (bf16[256,256]{1,0:T(8,128)(2,1)S(1)}, bf16[256,256]{1,0:T(8,128)(2,1)}, u32[]{:S(2)}, u32[]{:S(2)}) collective-permute-start(bf16[256,256]{1,0:T(8,128)(2,1)S(1)} %convolution_convert_fusion.1), channel_id=1, source_target_pairs={{8,0},{16,8},{24,16},{0,24},{9,1},{17,9},{25,17},{1,25},{10,2},{18... | collective-permute-start | bytes 393224 | tf_op jit(solution)/shard_map/ppermute | solution.py:21
  15.3 0.9 select_select_fusion
  16.3 6.5 %all-to-all-start = ((bf16[8,128,256]{2,1,0:T(8,128)(2,1)}), bf16[8,128,256]{2,1,0:T(8,128)(2,1)S(1)}, u32[]{:S(2)}, u32[]{:S(2)}) async-start(bf16[8,128,256]{2,1,0:T(8,128)(2,1)} %select_select_fusion), calls=%async_computation | async-start | bytes 1048576 | tf_op jit(solution)/shard_map/all_to_all | solution.py:80
  24.6 0.8 copy.20
  25.5 1.8 %gather_fusion.5 = bf16[256,256]{1,0:T(8,128)(2,1)} fusion(bf16[256,256]{1,0:T(8,128)(2,1)S(1)} %copy-done.2, s32[1024]{0:T(1024)S(1)} %pad_clamp_fusion.4), kind=kCustom, calls=%fused_computation.2.clone | custom fusion | bytes 263168 | tf_op jit(solution)/shard_map/jit(_take)/gather | solution.py:97
  27.4 2.0 %scatter_fusion = bf16[2,128,6,128]{3,1,2,0:T(8,128)(2,1)S(1)} fusion(bf16[2,128,6,128]{3,1,2,0:T(8,128)(2,1)S(1)} %broadcast_in_dim.61, s32[12]{0:T(128)S(1)} %fusion.42, bf16[12,128,128]{2,1,0:T(8,128)(2,1)} %param.24), kind=kCustom, calls=%fused_computation.7 | custom fusion | bytes 1179744 | tf_op jit(solution)/shard_map/scatter | solution.py:69
  29.5 1.1 copy.19
  31.1 1.7 %broadcast_multiply_fusion = bf16[40,2,128,128]{3,0,2,1:T(8,128)(2,1)} fusion(bf16[40,128,128]{2,0,1:T(8,128)(2,1)S(1)} %copy.20, bf16[40,2]{0,1:T(2,128)(2,1)S(1)} %fusion.38), kind=kLoop, calls=%fused_computation.21 | loop fusion | flops 1310720 | bytes 3932320 | tf_op jit(solution)/shard_map/rk,kab->rakb/dot_general | solution.py:87
  32.8 4.5 %all-to-all-done = bf16[8,128,256]{2,1,0:T(8,128)(2,1)S(1)} async-done(((bf16[8,128,256]{2,1,0:T(8,128)(2,1)}), bf16[8,128,256]{2,1,0:T(8,128)(2,1)S(1)}, u32[]{:S(2)}, u32[]{:S(2)}) %all-to-all-start) | async-done | bytes 524320 | tf_op jit(solution)/shard_map/all_to_all | solution.py:80
  37.3 0.7 gather_fusion.1
  38.4 1.4 copy-done.4
  39.8 0.8 fusion.1
  40.8 1.3 multiply_convert_fusion
  42.2 2.4 %gather_fusion.2 = bf16[40,128,256]{2,1,0:T(8,128)(2,1)} fusion(bf16[2,128,256]{2,1,0:T(8,128)(2,1)S(1)} %bitcast.74, s32[1024]{0:T(1024)S(1)} %pad_clamp_fusion), kind=kCustom, calls=%fused_computation.6 | custom fusion | bytes 5243040 | tf_op jit(solution)/shard_map/jit(_take)/gather | solution.py:114
  44.5 5.0 %fusion = (bf16[40,128,256]{1,2,0:T(8,128)(2,1)S(1)}, bf16[40,128,256]{1,2,0:T(8,128)(2,1)}) fusion(bf16[40,128,128]{2,1,0:T(8,128)(2,1)} %param.26, bf16[40,128,256]{2,1,0:T(8,128)(2,1)} %gather_fusion.2, pred[40]{0:T(512)(128)(4,1)S(1)} %copy-done.16), kind=kOutput, calls=%fused_computation.11 | convolution fusion | flops 342097920 | bytes 9175080 | tf_op jit(solution)/shard_map/kab,kaf->kbf/dot_general | solution.py:111
  49.5 4.7 %copy.22 = bf16[40,128,256]{2,0,1:T(8,128)(2,1)} copy(bf16[40,128,256]{1,2,0:T(8,128)(2,1)} %get-tuple-element.45) | data formatting | bytes 5242880 | tf_op jit(solution)/shard_map/convert_element_type | solution.py:29
  54.2 3.4 %copy.23 = bf16[40,128,256]{2,0,1:T(8,128)(2,1)} copy(bf16[40,128,256]{1,2,0:T(8,128)(2,1)S(1)} %get-tuple-element.44) | data formatting | bytes 5242880 | tf_op jit(solution)/shard_map/convert_element_type | solution.py:30
  57.6 2.5 %fusion.28 = f32[8,128,256]{2,0,1:T(8,128)S(1)} fusion(bf16[40,128,256]{2,0,1:T(8,128)(2,1)} %copy.22, s32[40]{0:T(128)S(1)} %get-tuple-element.50, pred[40]{0:T(512)(128)(4,1)S(1)} %copy-done.15), kind=kOutput, calls=%fused_computation.62 | convolution fusion | flops 20972160 | bytes 3670216 | tf_op jit(solution)/shard_map/rk,kaf->raf/dot_general | solution.py:32
  60.7 0.9 copy.24
  61.6 3.8 %all-to-all-start.1 = ((bf16[8,128,256]{2,1,0:T(8,128)(2,1)}), bf16[8,128,256]{2,1,0:T(8,128)(2,1)S(1)}, u32[]{:S(2)}, u32[]{:S(2)}) async-start(bf16[8,128,256]{2,1,0:T(8,128)(2,1)} %copy.24), calls=%async_computation.1 | async-start | bytes 1048576 | tf_op jit(solution)/shard_map/all_to_all | solution.py:120
  65.8 1.7 %collective-permute-start.3 = (bf16[256,256]{1,0:T(8,128)(2,1)S(1)}, bf16[256,256]{1,0:T(8,128)(2,1)S(1)}, u32[]{:S(2)}, u32[]{:S(2)}) collective-permute-start(bf16[256,256]{1,0:T(8,128)(2,1)S(1)} %get-tuple-element.47), channel_id=1, source_target_pairs={{8,0},{16,8},{24,16},{0,24},{9,1},{17,9},{25,17},{1,25},{10,2},{18... | collective-permute-start | bytes 393224 | tf_op jit(solution)/shard_map/ppermute | solution.py:21
  67.5 12.5 %all-to-all-done.1 = bf16[8,128,256]{2,1,0:T(8,128)(2,1)S(1)} async-done(((bf16[8,128,256]{2,1,0:T(8,128)(2,1)}), bf16[8,128,256]{2,1,0:T(8,128)(2,1)S(1)}, u32[]{:S(2)}, u32[]{:S(2)}) %all-to-all-start.1) | async-done | bytes 524320 | tf_op jit(solution)/shard_map/all_to_all | solution.py:120
  80.6 1.0 fusion.24
  81.7 1.4 scatter_custom_fusion.1
  83.1 1.2 gather_fusion.4
  84.5 1.2 gather_fusion.6
  85.6 0.8 broadcast_select_fusion.1
  86.4 70.9 %all-gather.3.cloned.1.call-done = f32[8192,256]{1,0:T(8,128)} async-done(((f32[256,256]{1,0:T(8,128)}), f32[8192,256]{1,0:T(8,128)}) %all-gather.3.cloned.1.call-update) | async-done | bytes 8388624 | tf_op jit(solution)/shard_map/all_gather | solution.py:8
  157.3 3.9 %reduce_sum.9 = f32[256,256]{1,0:T(8,128)S(1)} reduce(f32[32,256,256]{2,1,0:T(8,128)} %bitcast.75, f32[]{:T(128)} %constant.141.clone.1), dimensions={0}, to_apply=%region_2.4 | reduce | flops 2031616 | bytes 8650756 | tf_op jit(solution)/shard_map/reduce_sum | solution.py:7
  161.3 0.7 broadcast_multiply_fusion.1
  (77 shorter events, 7.4 us)
Async XLA Ops:
  7.2 3.4 %copy-start = (bf16[256,256]{1,0:T(8,128)(2,1)S(1)}, bf16[256,256]{1,0:T(8,128)(2,1)}, u32[]{:S(2)}) copy-start(bf16[256,256]{1,0:T(8,128)(2,1)} %param.22) | copy-start | bytes 393220
  7.2 15.6 %copy-start.9 = (s32[40,2]{0,1:T(2,128)S(1)}, s32[40,2]{0,1:T(2,128)}, u32[]{:S(2)}) copy-start(s32[40,2]{0,1:T(2,128)} %param.27) | copy-start | bytes 964
  7.2 16.8 %copy-start.20 = (s32[12,2]{0,1:T(2,128)S(1)}, s32[12,2]{0,1:T(2,128)}, u32[]{:S(2)}) copy-start(s32[12,2]{0,1:T(2,128)} %param.25) | copy-start | bytes 292
  7.2 17.4 %copy-start.3 = (bf16[40,128,128]{2,1,0:T(8,128)(2,1)S(1)}, bf16[40,128,128]{2,1,0:T(8,128)(2,1)}, u32[]{:S(2)}) copy-start(bf16[40,128,128]{2,1,0:T(8,128)(2,1)} %param.26) | copy-start | bytes 3932164
  8.7 5.3 %copy-start.12 = (pred[256]{0:T(512)(128)(4,1)}, pred[256]{0:T(512)(128)(4,1)S(1)}, u32[]{:S(2)}) copy-start(pred[256]{0:T(512)(128)(4,1)S(1)} %compare_and_fusion.1) | copy-start | bytes 772
  10.6 4.1 %copy-start.6 = (bf16[256,256]{1,0:T(8,128)(2,1)}, bf16[256,256]{1,0:T(8,128)(2,1)S(1)}, u32[]{:S(2)}) copy-start(bf16[256,256]{1,0:T(8,128)(2,1)S(1)} %gather_fusion.3) | copy-start | bytes 393220
  10.9 29.8 %collective-permute-start = (bf16[256,256]{1,0:T(8,128)(2,1)S(1)}, bf16[256,256]{1,0:T(8,128)(2,1)}, u32[]{:S(2)}, u32[]{:S(2)}) collective-permute-start(bf16[256,256]{1,0:T(8,128)(2,1)S(1)} %convolution_convert_fusion.1), channel_id=1, source_target_pairs={{0,8},{8,16},{16,24},{24,0},{1,9},{9,17},{17,25},{25,1},{2,10},{10... | collective-permute-start | bytes 393224 | tf_op jit(solution)/shard_map/ppermute | solution.py:19
  11.4 29.3 %collective-permute-start.1 = (bf16[256,256]{1,0:T(8,128)(2,1)S(1)}, bf16[256,256]{1,0:T(8,128)(2,1)}, u32[]{:S(2)}, u32[]{:S(2)}) collective-permute-start(bf16[256,256]{1,0:T(8,128)(2,1)S(1)} %convolution_convert_fusion.1), channel_id=1, source_target_pairs={{8,0},{16,8},{24,16},{0,24},{9,1},{17,9},{25,17},{1,25},{10,2},{18... | collective-permute-start | bytes 393224 | tf_op jit(solution)/shard_map/ppermute | solution.py:21
  15.3 10.2 %copy-start.2 = (bf16[256,256]{1,0:T(8,128)(2,1)S(1)}, bf16[256,256]{1,0:T(8,128)(2,1)}, u32[]{:S(2)}) copy-start(bf16[256,256]{1,0:T(8,128)(2,1)} %param.23) | copy-start | bytes 393220
  16.3 21.1 %all-to-all-start = ((bf16[8,128,256]{2,1,0:T(8,128)(2,1)}), bf16[8,128,256]{2,1,0:T(8,128)(2,1)S(1)}, u32[]{:S(2)}, u32[]{:S(2)}) async-start(bf16[8,128,256]{2,1,0:T(8,128)(2,1)} %select_select_fusion), calls=%async_computation | async-start | bytes 1048576 | tf_op jit(solution)/shard_map/all_to_all | solution.py:80
  25.5 5.1 %copy-start.17 = (s32[40]{0:T(128)S(1)}, s32[40]{0:T(128)}, u32[]{:S(2)}) copy-start(s32[40]{0:T(128)} %get-tuple-element.51) | copy-start | bytes 484
  25.5 5.1 %copy-start.14 = (pred[40]{0:T(512)(128)(4,1)S(1)}, pred[40]{0:T(512)(128)(4,1)}, u32[]{:S(2)}) copy-start(pred[40]{0:T(512)(128)(4,1)} %iota_compare_fusion.1) | copy-start | bytes 124
  25.5 5.1 %copy-start.18 = (s32[40]{0:T(128)S(1)}, s32[40]{0:T(128)}, u32[]{:S(2)}) copy-start(s32[40]{0:T(128)} %get-tuple-element.53) | copy-start | bytes 484
  25.5 5.1 %copy-start.10 = (s32[40,2]{0,1:T(2,128)S(1)}, s32[40,2]{0,1:T(2,128)}, u32[]{:S(2)}) copy-start(s32[40,2]{0,1:T(2,128)} %param.27) | copy-start | bytes 964
  38.0 1.7 %copy-start.4 = (bf16[40,2,128,128]{3,0,2,1:T(8,128)(2,1)S(1)}, bf16[40,2,128,128]{3,0,2,1:T(8,128)(2,1)}, u32[]{:S(2)}) copy-start(bf16[40,2,128,128]{3,0,2,1:T(8,128)(2,1)} %broadcast_multiply_fusion) | copy-start | bytes 7864324
  39.8 1.0 copy-start.5
  39.8 1.0 copy-start.8
  39.8 1.0 copy-start.13
  42.2 2.4 %copy-start.16 = (pred[40]{0:T(512)(128)(4,1)S(1)}, pred[40]{0:T(512)(128)(4,1)}, u32[]{:S(2)}) copy-start(pred[40]{0:T(512)(128)(4,1)} %get-tuple-element.54) | copy-start | bytes 124
  54.2 3.4 %copy-start.15 = (pred[40]{0:T(512)(128)(4,1)S(1)}, pred[40]{0:T(512)(128)(4,1)}, u32[]{:S(2)}) copy-start(pred[40]{0:T(512)(128)(4,1)} %iota_compare_fusion.1) | copy-start | bytes 124
  57.6 2.5 %copy-start.1 = (bf16[40,128,256]{2,0,1:T(8,128)(2,1)S(1)}, bf16[40,128,256]{2,0,1:T(8,128)(2,1)}, u32[]{:S(2)}) copy-start(bf16[40,128,256]{2,0,1:T(8,128)(2,1)} %copy.23) | copy-start | bytes 7864324
  60.7 19.3 %copy-start.19 = (s32[1,8]{1,0:T(1,128)S(1)}, s32[1,8]{1,0:T(1,128)}, u32[]{:S(2)}) copy-start(s32[1,8]{1,0:T(1,128)} %param.29) | copy-start | bytes 100
  61.6 19.0 %copy-start.7 = (bf16[256,256]{1,0:T(8,128)(2,1)S(1)}, bf16[256,256]{1,0:T(8,128)(2,1)}, u32[]{:S(2)}) copy-start(bf16[256,256]{1,0:T(8,128)(2,1)} %copy-done.6) | copy-start | bytes 393220
  61.6 18.4 %all-to-all-start.1 = ((bf16[8,128,256]{2,1,0:T(8,128)(2,1)}), bf16[8,128,256]{2,1,0:T(8,128)(2,1)S(1)}, u32[]{:S(2)}, u32[]{:S(2)}) async-start(bf16[8,128,256]{2,1,0:T(8,128)(2,1)} %copy.24), calls=%async_computation.1 | async-start | bytes 1048576 | tf_op jit(solution)/shard_map/all_to_all | solution.py:120
  65.4 16.2 %copy-start.11 = (s32[1,256]{1,0:T(1,128)S(1)}, s32[1,256]{1,0:T(1,128)}, u32[]{:S(2)}) copy-start(s32[1,256]{1,0:T(1,128)} %param.30) | copy-start | bytes 3076
  65.4 91.9 %all-gather.3.cloned.1.call-start = ((), (), s32[]{:S(2)}) async-start(), calls=%async_computation.2 | async-start | bytes 8650752 | tf_op jit(solution)/shard_map/all_gather | solution.py:8
  65.7 14.8 %collective-permute-start.2 = (bf16[256,256]{1,0:T(8,128)(2,1)S(1)}, bf16[256,256]{1,0:T(8,128)(2,1)S(1)}, u32[]{:S(2)}, u32[]{:S(2)}) collective-permute-start(bf16[256,256]{1,0:T(8,128)(2,1)S(1)} %get-tuple-element.46), channel_id=1, source_target_pairs={{0,8},{8,16},{16,24},{24,0},{1,9},{9,17},{17,25},{25,1},{2,10},{10... | collective-permute-start | bytes 393224 | tf_op jit(solution)/shard_map/ppermute | solution.py:19
  65.8 14.7 %collective-permute-start.3 = (bf16[256,256]{1,0:T(8,128)(2,1)S(1)}, bf16[256,256]{1,0:T(8,128)(2,1)S(1)}, u32[]{:S(2)}, u32[]{:S(2)}) collective-permute-start(bf16[256,256]{1,0:T(8,128)(2,1)S(1)} %get-tuple-element.47), channel_id=1, source_target_pairs={{8,0},{16,8},{24,16},{0,24},{9,1},{17,9},{25,17},{1,25},{10,2},{18... | collective-permute-start | bytes 393224 | tf_op jit(solution)/shard_map/ppermute | solution.py:21
Sparse Core Ops, SparseCore 0:
  81.7 75.5 all-gather.2
